TPU v7x, 32 devices: a whole 2x2x4 slice. The times are simulated.
32 devices in a mesh: bucket: 8 (over z, x), rel: 4 (over y, core).
Axes of the slice: x: 2, y: 2, z: 4, core: 2. Of those that a mesh axis runs over, the one named last changes fastest.
Arguments:
- left_rows: float32 [8192, 512], P(('bucket', 'rel')), may hold values from -1.2 to 1.2
- left_state: float32 [8192], P(('bucket', 'rel')), may hold values from 1e-06 to 0.0001
- right_rows: float32 [8192, 512], P(('bucket', 'rel')), may hold values from -1.2 to 1.2
- right_state: float32 [8192], P(('bucket', 'rel')), may hold values from 1e-06 to 0.0001
- relations: bfloat16 [4, 512, 512], P('rel'), may hold values from -0.25 to 0.25
- fetch_ids: int32 [8, 4, 4], P('bucket', 'rel'), may hold values from 0 to 3
- edge_left: int32 [8, 4, 2, 512], P('bucket', 'rel'), may hold values from 0 to 255
- edge_right: int32 [8, 4, 2, 512], P('bucket', 'rel'), may hold values from 0 to 255
- edge_slot: int32 [8, 4, 2, 512], P('bucket', 'rel'), may hold values from 0 to 1
- edge_weight: int32 [8, 4, 2, 512], P('bucket', 'rel'), may hold values from 1 to 4
- matching: int32 [1], replicated, may hold values from 1 to 7
Outputs:
- left_out: float32 [8192, 512], P(('bucket', 'rel'))
- left_state_out: float32 [8192], P(('bucket', 'rel'))
- right_out: float32 [8192, 512], P(('bucket', 'rel'))
- right_state_out: float32 [8192], P(('bucket', 'rel'))
- rel_grad: float32 [4, 512, 512], P('rel')
Inputs may be any that keep to these rules, and one draw needn't show every extreme that they name: Bucket b is paired with bucket b XOR matching.
All inputs are finite; a program needn't handle non-finite values.
Results may differ from a plain program's by a relative error of at most 0.0015.
The roundings to bfloat16 on the way count: a program that leaves them out, or rounds other values in their place, can miss the bound.
Values may be sent and summed in bfloat16 or wider, within the bound.
No kernel may reach another device: no remote copies, remote signals or barrier semaphores. Data moves between devices by JAX's collectives and lax.ppermute only.
A program may use at most 64 MiB of HBM per device.

v0:
```python
import jax
import jax.numpy as jnp
from jax import lax
from jax.sharding import PartitionSpec as P

learn_rate = 0.1


def edge_targets(edge_left, edge_right, edge_slot, edge_weight, block_len):
    table = jnp.zeros((2, block_len, block_len), jnp.float32)
    table = table.at[edge_slot, edge_left, edge_right].add(edge_weight.astype(jnp.float32))
    return [table[0], table[1]]


def adagrad(table, state, gradient):
    state_new = state + jnp.mean(gradient * gradient, axis=1)
    return (table - learn_rate * gradient / jnp.sqrt(state_new)[:, None], state_new)


def one_round(
    left_block,
    left_st,
    right_block,
    right_st,
    rel_pair,
    edge_left,
    edge_right,
    edge_slot,
    edge_weight,
):
    block_len = left_block.shape[0]
    left_half = left_block.astype(jnp.bfloat16)
    right_half = right_block.astype(jnp.bfloat16)
    targets = edge_targets(edge_left, edge_right, edge_slot, edge_weight, block_len)
    grad_left = jnp.zeros(left_block.shape, jnp.float32)
    grad_right = jnp.zeros(right_block.shape, jnp.float32)
    rel_grads = []
    for slot_index in range(2):
        matrix = rel_pair[slot_index]
        projected = jnp.dot(left_half, matrix, preferred_element_type=jnp.float32).astype(
            jnp.bfloat16
        )
        scores = jnp.dot(projected, right_half.T, preferred_element_type=jnp.float32)
        score_grad = ((jax.nn.sigmoid(scores) - targets[slot_index]) / block_len).astype(
            jnp.bfloat16
        )
        carried = jnp.dot(score_grad, right_half, preferred_element_type=jnp.float32).astype(
            jnp.bfloat16
        )
        grad_left = grad_left + jnp.dot(carried, matrix.T, preferred_element_type=jnp.float32)
        grad_right = grad_right + jnp.dot(
            score_grad.T, projected, preferred_element_type=jnp.float32
        )
        rel_grads.append(jnp.dot(left_half.T, carried, preferred_element_type=jnp.float32))
    left_new, left_st_new = adagrad(left_block, left_st, grad_left)
    right_new, right_st_new = adagrad(right_block, right_st, grad_right)
    return (left_new, left_st_new, right_new, right_st_new, rel_grads)


def partner_blocks(row_block, state_block, switch):
    block_len = row_block.shape[0]
    width = row_block.shape[1]
    partner = jnp.bitwise_xor(lax.axis_index("bucket"), switch)
    portion = (
        lax.all_gather(row_block, "bucket", axis=0, tiled=True),
        lax.all_gather(state_block, "bucket", axis=0, tiled=True),
    )
    block_count = portion[0].shape[0] // block_len
    owners = jnp.arange(block_count, dtype=jnp.int32)
    chosen = owners == partner
    rows_part = portion[0].reshape(block_count, block_len, width)
    states_part = portion[1].reshape(block_count, block_len)
    rows_new = jnp.sum(jnp.where(chosen[:, None, None], rows_part, jnp.float32(0.0)), axis=0)
    states_new = jnp.sum(jnp.where(chosen[:, None], states_part, jnp.float32(0.0)), axis=0)
    return (rows_new, states_new)


def reduce_gradients(gradients, rel_ids, rel_total, width):
    stacked = jnp.stack(gradients)
    own_rows = rel_total // lax.axis_size("rel") * width
    rel_count_piece = own_rows * lax.axis_size("rel") // width
    rel_list = jnp.arange(rel_count_piece, dtype=jnp.int32)
    weights = (rel_ids[:, None] == rel_list[None, :]).astype(jnp.float32)
    term = jnp.einsum("sk,sde->kde", weights, stacked, precision=lax.Precision.HIGHEST)
    partial_sum = lax.psum_scatter(
        term.reshape(rel_count_piece * width, width), "rel", scatter_dimension=0, tiled=True
    )
    return lax.psum(partial_sum, "bucket")


def on_device(
    left_rows,
    left_state,
    right_rows,
    right_state,
    relations,
    fetch_ids,
    edge_left,
    edge_right,
    edge_slot,
    edge_weight,
    matching,
):
    width = relations.shape[1]
    rel_table = lax.all_gather(relations, "rel", axis=0, tiled=True)
    rel_total = rel_table.shape[0]
    rel_ids = fetch_ids[0, 0]
    switch = matching[0]
    table_left, state_left = (left_rows, left_state)
    row_block, state_block = (right_rows, right_state)
    gradients = []
    for round_index in range(2):
        rel_pair = jnp.take(rel_table, rel_ids[2 * round_index : 2 * round_index + 2], axis=0)
        table_left, state_left, row_block, state_block, rel_grads = one_round(
            table_left,
            state_left,
            row_block,
            state_block,
            rel_pair,
            edge_left[0, 0, round_index],
            edge_right[0, 0, round_index],
            edge_slot[0, 0, round_index],
            edge_weight[0, 0, round_index],
        )
        gradients.extend(rel_grads)
        if round_index == 0:
            row_block, state_block = partner_blocks(row_block, state_block, switch)
    owned = reduce_gradients(gradients, rel_ids, rel_total, width)
    return (table_left, state_left, row_block, state_block, owned.reshape(-1, width, width))


def solution(mesh):
    in_specs = (
        P(("bucket", "rel"), None),
        P(("bucket", "rel")),
        P(("bucket", "rel"), None),
        P(("bucket", "rel")),
        P("rel", None, None),
        P("bucket", "rel", None),
        P("bucket", "rel", None, None),
        P("bucket", "rel", None, None),
        P("bucket", "rel", None, None),
        P("bucket", "rel", None, None),
        P(),
    )
    out_specs = (
        P(("bucket", "rel"), None),
        P(("bucket", "rel")),
        P(("bucket", "rel"), None),
        P(("bucket", "rel")),
        P("rel", None, None),
    )
    return jax.shard_map(
        on_device, mesh=mesh, in_specs=in_specs, out_specs=out_specs, check_vma=False
    )
```

profile of v0, /device:TPU:0, one launch (start us, length us, event | category | flops | bytes accessed | tf_op | source)
XLA Modules:
  0.0 281.4 jit_solution(3566939604815437510)
XLA Ops:
  7.2 0.0 all-gather.4.cloned.1.call-start
  7.2 0.7 all-gather.4.cloned.1.call-update
  7.9 0.0 all-gather.6.cloned.1.call-start
  8.0 1.1 convert_element_type.65
  9.0 1.1 convert_element_type.63
  10.1 0.8 slice_convert_fusion
  10.9 0.8 or_select_fusion
  11.7 31.3 %scatter_fusion = f32[2,256,256]{2,1,0:T(8,128)S(1)} fusion(f32[2,256,256]{2,1,0:T(8,128)S(1)} %broadcast.145.clone, s32[512]{0:T(512)S(1)} %bitcast.126, f32[512]{0:T(512)S(1)} %bitcast.131), kind=kCustom, calls=%fused_computation.2 | custom fusion | flops 512 | bytes 12288 | tf_op jit(solution)/shard_map/scatter-add | solution.py:11
  43.1 0.6 compare_and_fusion
  43.7 2.2 gather_fusion
  45.9 0.2 broadcast_select_fusion.1
  46.1 0.3 convolution_convert_fusion.5
  46.5 0.3 convolution_convert_fusion.7
  46.8 0.3 fusion.22
  47.1 0.3 fusion.23
  47.4 0.3 fusion.40
  47.7 0.4 multiply_reduce_fusion.2
  48.0 0.6 fusion.39
  48.6 0.9 divide_subtract_fusion.2
  49.5 0.0 all-gather.6.cloned.1.call-update
  49.6 0.2 reduce-scatter.2.cloned.1.call-start
  50.5 31.3 %scatter_fusion.1 = f32[2,256,256]{2,1,0:T(8,128)S(1)} fusion(f32[2,256,256]{2,1,0:T(8,128)S(1)} %broadcast.145.clone.1, s32[512]{0:T(512)S(1)} %bitcast.125, f32[512]{0:T(512)S(1)} %bitcast.130), kind=kCustom, calls=%fused_computation.3 | custom fusion | flops 512 | bytes 12288 | tf_op jit(solution)/shard_map/scatter-add | solution.py:11
  81.8 0.5 iota_compare_fusion.1
  82.3 3.2 %gather_fusion.1 = bf16[2,512,512]{2,1,0:T(8,128)(2,1)} fusion(bf16[4,512,512]{2,1,0:T(8,128)(2,1)} %all-gather.4.cloned.1.call-done, s32[1024]{0:T(1024)S(1)} %get-tuple-element.30), kind=kCustom, calls=%fused_computation.1.clone | custom fusion | bytes 2097160 | tf_op jit(solution)/shard_map/jit(_take)/gather | solution.py:113
  85.5 0.2 convolution_convert_fusion.4
  85.8 1.3 convolution_bitcast_fusion.2
  87.1 0.2 convolution_convert_fusion.6
  87.3 1.3 convolution_bitcast_fusion.3
  88.6 0.3 fusion.24
  88.9 0.4 multiply_reduce_fusion.3
  89.4 0.1 fusion.36
  89.6 0.2 broadcast_select_fusion
  89.7 0.3 convolution_convert_fusion.1
  90.0 1.0 convolution_convert_fusion.3
  91.1 34.1 %all-gather.6.cloned.1.call-done = f32[2048,512]{1,0:T(8,128)} async-done(((f32[256,512]{1,0:T(8,128)}), f32[2048,512]{1,0:T(8,128)}) %all-gather.6.cloned.1.call-update) | async-done | bytes 4194320 | tf_op jit(solution)/shard_map/all_gather | solution.py:65
  125.2 2.9 %select_reduce_fusion = f32[256,512]{1,0:T(8,128)S(1)} fusion(f32[8,256,512]{2,1,0:T(8,128)} %bitcast.128, pred[8]{0:T(512)(128)(4,1)S(1)} %copy-done.14), kind=kLoop, calls=%fused_computation.5 | loop fusion | flops 1966080 | bytes 4718600 | tf_op jit(solution)/shard_map/reduce_sum | solution.py:73
  128.1 0.3 fusion.20
  128.4 0.2 convolution_convert_fusion
  128.7 0.3 fusion.21
  129.0 0.2 convolution_convert_fusion.2
  129.2 0.4 copy-done.7
  129.6 0.3 convolution_bitcast_fusion
  130.0 0.3 convolution_bitcast_fusion.1
  130.3 2.4 pad_maximum_fusion
  132.7 5.5 %copy.25 = f32[4,512,512]{2,0,1:T(4,128)} copy(f32[4,512,512]{1,2,0:T(8,128)} %pad_maximum_fusion) | data formatting | bytes 8388608 | tf_op jit(solution)/shard_map/stack | solution.py:79
  138.2 6.2 %fusion.32 = f32[4,512,512]{2,0,1:T(4,128)S(1)} fusion(f32[4,512,512]{2,0,1:T(4,128)} %copy.25, s32[4]{0:T(128)S(1)} %bitcast.132), kind=kOutput, calls=%fused_computation.98 | convolution fusion | flops 50331664 | bytes 8388624 | tf_op jit(solution)/shard_map/sk,sde->kde/dot_general | solution.py:84
  144.4 3.2 %copy.26 = f32[4,512,512]{2,1,0:T(8,128)} copy(f32[4,512,512]{2,0,1:T(4,128)S(1)} %fusion.32) | data formatting | bytes 8388608 | tf_op jit(solution)/shard_map/sk,sde->kde/dot_general | solution.py:84
  147.7 0.0 reduce-scatter.2.cloned.1.call-update
  147.7 0.0 all-reduce.2.cloned.1.call-start
  147.7 0.6 copy-done.13
  148.3 18.1 %all-gather = f32[8,1,256]{2,1,0:T(1,128)S(1)} all-gather(f32[1,1,256]{2,1,0:T(1,128)S(1)} %bitcast.133), channel_id=1, replica_groups=mesh['bucket'=8,'rel'=4] {'bucket'}, dimensions={0}, use_global_device_ids=true | all-gather | bytes 9216 | tf_op jit(solution)/shard_map/all_gather | solution.py:66
  166.5 0.1 fusion.26
  166.5 1.2 fusion.41
  167.7 1.1 fusion.25
  168.9 2.0 multiply_reduce_fusion
  170.9 20.1 %reduce-scatter.2.cloned.1.call-done = f32[512,512]{1,0:T(8,128)} async-done(((f32[2048,512]{1,0:T(8,128)}), f32[512,512]{1,0:T(8,128)}) %reduce-scatter.2.cloned.1.call-update) | async-done | bytes 1048592 | tf_op jit(solution)/shard_map/reduce_scatter | solution.py:85
  191.0 0.0 all-reduce.2.cloned.1.call-update
  191.0 0.6 fusion.37
  191.6 1.5 multiply_reduce_fusion.1
  193.0 0.6 fusion.38
  193.6 2.0 divide_subtract_fusion
  195.5 1.0 divide_subtract_fusion.1
  196.6 76.1 %all-reduce.2.cloned.1.call-done = f32[1,512,512]{2,1,0:T(8,128)} async-done(((f32[1,512,512]{2,1,0:T(8,128)}), f32[1,512,512]{2,1,0:T(8,128)}) %all-reduce.2.cloned.1.call-update) | async-done | bytes 1048592 | tf_op jit(solution)/shard_map/psum | solution.py:88
  272.6 2.3 copy.35
  (40 shorter events, 0.2 us)
Async XLA Ops:
  7.2 35.9 %copy-start.11 = (s32[1,1,4]{2,1,0:T(1,128)S(1)}, s32[1,1,4]{2,1,0:T(1,128)}, u32[]{:S(2)}) copy-start(s32[1,1,4]{2,1,0:T(1,128)} %param.18) | copy-start | bytes 52
  7.2 36.5 %all-gather.4.cloned.1.call-start = ((), (), s32[]{:S(2)}) async-start(), calls=%async_computation.1 | async-start | bytes 2621440 | tf_op jit(solution)/shard_map/all_gather | solution.py:105
  7.9 117.3 %all-gather.6.cloned.1.call-start = ((), (), s32[]{:S(2)}) async-start(), calls=%async_computation.2 | async-start | bytes 4718592 | tf_op jit(solution)/shard_map/all_gather | solution.py:65
  46.1 2.0 copy-start.17
  46.1 2.5 copy-start.6
  49.6 141.4 %reduce-scatter.2.cloned.1.call-start = ((), (), s32[]{:S(2)}) async-start(), calls=%async_computation.3 | async-start | bytes 5242880 | tf_op jit(solution)/shard_map/reduce_scatter | solution.py:85
  85.5 3.9 %copy-start.12 = (f32[256]{0:T(256)S(1)}, f32[256]{0:T(256)}, u32[]{:S(2)}) copy-start(f32[256]{0:T(256)} %param.14) | copy-start | bytes 3076
  85.5 3.9 %copy-start = (f32[256,512]{1,0:T(8,128)S(1)}, f32[256,512]{1,0:T(8,128)}, u32[]{:S(2)}) copy-start(f32[256,512]{1,0:T(8,128)} %param.13) | copy-start | bytes 1572868
  85.7 3.8 %copy-start.1 = (bf16[2,512,512]{2,1,0:T(8,128)(2,1)S(1)}, bf16[2,512,512]{2,1,0:T(8,128)(2,1)}, u32[]{:S(2)}) copy-start(bf16[2,512,512]{2,1,0:T(8,128)(2,1)} %gather_fusion.1) | copy-start | bytes 3145732
  85.8 3.8 %copy-start.16 = (pred[2]{0:T(512)(128)(4,1)S(1)}, pred[2]{0:T(512)(128)(4,1)}, u32[]{:S(2)}) copy-start(pred[2]{0:T(512)(128)(4,1)} %get-tuple-element.12) | copy-start | bytes 10
  88.6 36.6 %copy-start.14 = (pred[8]{0:T(512)(128)(4,1)S(1)}, pred[8]{0:T(512)(128)(4,1)}, u32[]{:S(2)}) copy-start(pred[8]{0:T(512)(128)(4,1)} %iota_compare_fusion.1) | copy-start | bytes 28
  89.5 35.7 %copy-start.4 = (bf16[256,512]{1,0:T(8,128)(2,1)}, bf16[256,512]{1,0:T(8,128)(2,1)S(1)}, u32[]{:S(2)}) copy-start(bf16[256,512]{1,0:T(8,128)(2,1)S(1)} %fusion.36) | copy-start | bytes 786436
  90.0 38.1 %copy-start.9 = (bf16[256,512]{1,0:T(8,128)(2,1)}, bf16[256,512]{1,0:T(8,128)(2,1)S(1)}, u32[]{:S(2)}) copy-start(bf16[256,512]{1,0:T(8,128)(2,1)S(1)} %convolution_convert_fusion.1) | copy-start | bytes 786436
  125.2 3.5 %copy-start.10 = (bf16[256,512]{1,0:T(8,128)(2,1)S(1)}, bf16[256,512]{1,0:T(8,128)(2,1)}, u32[]{:S(2)}) copy-start(bf16[256,512]{1,0:T(8,128)(2,1)} %convolution_convert_fusion.3) | copy-start | bytes 786436
  125.2 4.4 %copy-start.5 = (bf16[256,512]{1,0:T(8,128)(2,1)S(1)}, bf16[256,512]{1,0:T(8,128)(2,1)}, u32[]{:S(2)}) copy-start(bf16[256,512]{1,0:T(8,128)(2,1)} %copy-done.4) | copy-start | bytes 786436
  128.1 2.3 copy-start.2
  128.1 2.3 copy-start.3
  129.0 0.7 copy-start.7
  147.7 0.7 copy-start.13
  147.7 18.8 %copy-start.15 = (pred[8]{0:T(512)(128)(4,1)S(1)}, pred[8]{0:T(512)(128)(4,1)}, u32[]{:S(2)}) copy-start(pred[8]{0:T(512)(128)(4,1)} %iota_compare_fusion.1) | copy-start | bytes 28
  147.7 18.9 %copy-start.8 = (bf16[256,256]{1,0:T(8,128)(2,1)S(1)}, bf16[256,256]{1,0:T(8,128)(2,1)}, u32[]{:S(2)}) copy-start(bf16[256,256]{1,0:T(8,128)(2,1)} %copy-done.7) | copy-start | bytes 393220
  147.7 124.9 %all-reduce.2.cloned.1.call-start = ((), (), s32[]{:S(2)}) async-start(), calls=%async_computation.4 | async-start | bytes 2097152 | tf_op jit(solution)/shard_map/psum | solution.py:88
Sparse Core Ops, SparseCore 0:
  9.5 25.2 all-gather.3
  49.7 75.4 all-gather.5
  147.8 43.1 reduce-scatter.1
  194.3 78.2 all-reduce.1
where the time goes:
time: 282 us; the launch traced here: 281 us
  waiting for transfers between devices  131 us (46%)
  other arithmetic  79 us (28%)
  matrix products  20.7 us (7%)
  blocking collectives  18.1 us (6%)
  local copies, waits for them, and re-layouts  17.5 us (6%)
  between operations  14.8 us (5%)
    psum x1, waiting for transfers between devices, reduce_gradients(): return lax.psum(partial_sum, 'bucket')  76.1 us
    scatter-add x2, other arithmetic, edge_targets(): table.at[edge_slot, edge_left, edge_right]  62.7 us
    all_gather x1, waiting for transfers between devices, partner_blocks(): lax.all_gather(row_block, 'bucket', axis=0, tiled=True)  34.1 us
    reduce_scatter x1, waiting for transfers between devices, reduce_gradients(): lax.psum_scatter(term.reshape(rel_count_piece * width, width), 'rel', sca...  20.1 us
    all_gather x1, blocking collectives, partner_blocks(): lax.all_gather(state_block, 'bucket', axis=0, tiled=True)  18.1 us
    dot_general x1, matrix products, reduce_gradients(): jnp.einsum('sk,sde->kde', weights, stacked, precision=lax.Precision.HIGHEST)  6.2 us
  transfers between devices with their start and end apart: 4, of which 3 were waited for; matrix products, arithmetic and copies ran while one was open for 31% of the time, Pallas kernels for 0%

commit v1 on v0

--- a/solution.py
+++ b/solution.py
@@ -85,7 +85,11 @@
     partial_sum = lax.psum_scatter(
         term.reshape(rel_count_piece * width, width), "rel", scatter_dimension=0, tiled=True
     )
-    return lax.psum(partial_sum, "bucket")
+
+    def part_the_outputs(q_in):
+        return jnp.sum(jax.lax.all_gather(q_in, "bucket"), axis=0)
+
+    return part_the_outputs(partial_sum)
 
 
 def on_device(

time: 282 us -> 330 us (1.17)
  waiting for transfers between devices: 131 us -> 177 us
  other arithmetic: 79 us -> 83.5 us
  local copies, waits for them, and re-layouts: 17.5 us -> 14.2 us
    all_gather x0 -> x1, waiting for transfers between devices: none -> 98.9 us  [part_the_outputs(): return jnp.sum(jax.lax.all_gather(q_in, 'bucket'), axis=0)]
    psum x1 -> x0, waiting for transfers between devices: 76.1 us -> none  [reduce_gradients(): return lax.psum(partial_sum, 'bucket')]
    reduce_scatter x1, waiting for transfers between devices: 20.1 us -> 43.2 us  [reduce_gradients(): lax.psum_scatter(term.reshape(rel_count_piece * width, width), 'rel', sca...]
    reduce_sum x0 -> x1, other arithmetic: none -> 5.46 us  [part_the_outputs(): return jnp.sum(jax.lax.all_gather(q_in, 'bucket'), axis=0)]
  transfers between devices with their start and end apart: 4 -> 4, of which waited for: 3 -> 3; matrix products, arithmetic and copies ran while one was open for 31% -> 25% of each run, Pallas kernels for 0% -> 0%
where the time goes in v1:
time: 330 us; the launch traced here: 329 us
  waiting for transfers between devices  177 us (54%)
  other arithmetic  83.5 us (25%)
  blocking collectives  21.1 us (6%)
  matrix products  18.1 us (5%)
  between operations  14.8 us (4%)
  local copies, waits for them, and re-layouts  14.2 us (4%)
    all_gather x1, waiting for transfers between devices, part_the_outputs(): return jnp.sum(jax.lax.all_gather(q_in, 'bucket'), axis=0)  98.9 us
    scatter-add x2, other arithmetic, edge_targets(): table.at[edge_slot, edge_left, edge_right]  62.7 us
    reduce_scatter x1, waiting for transfers between devices, reduce_gradients(): lax.psum_scatter(term.reshape(rel_count_piece * width, width), 'rel', sca...  43.2 us
    all_gather x1, waiting for transfers between devices, partner_blocks(): lax.all_gather(row_block, 'bucket', axis=0, tiled=True)  34.1 us
    all_gather x1, blocking collectives, partner_blocks(): lax.all_gather(state_block, 'bucket', axis=0, tiled=True)  21.1 us
  transfers between devices with their start and end apart: 4, of which 3 were waited for; matrix products, arithmetic and copies ran while one was open for 25% of the time, Pallas kernels for 0%

profile of v1, /device:TPU:0, one launch (start us, length us, event | category | flops | bytes accessed | tf_op | source)
XLA Modules:
  0.0 329.0 jit_solution(6200558762393507346)
XLA Ops:
  7.2 0.0 all-gather.6.cloned.1.call-start
  7.2 0.7 all-gather.6.cloned.1.call-update
  7.9 0.0 all-gather.8.cloned.1.call-start
  8.0 1.1 convert_element_type.63
  9.0 1.1 convert_element_type.65
  10.1 0.8 slice_convert_fusion
  10.9 0.8 or_select_fusion
  11.7 31.3 %scatter_fusion = f32[2,256,256]{2,1,0:T(8,128)S(1)} fusion(f32[2,256,256]{2,1,0:T(8,128)S(1)} %broadcast.145.clone, s32[512]{0:T(512)S(1)} %bitcast.127, f32[512]{0:T(512)S(1)} %bitcast.133), kind=kCustom, calls=%fused_computation.2 | custom fusion | flops 512 | bytes 12288 | tf_op jit(solution)/shard_map/scatter-add | solution.py:11
  43.1 0.6 compare_and_fusion
  43.7 2.2 gather_fusion
  45.9 0.2 broadcast_select_fusion.1
  46.1 0.0 copy-start.6
  46.1 0.3 convolution_convert_fusion.7
  46.5 0.3 convolution_convert_fusion.5
  46.8 0.3 fusion.23
  47.1 0.3 fusion.22
  47.4 0.3 fusion.40
  47.7 0.4 multiply_reduce_fusion.2
  48.0 0.6 fusion.39
  48.6 0.9 divide_subtract_fusion.2
  49.5 0.0 all-gather.8.cloned.1.call-update
  49.6 0.2 reduce-scatter.2.cloned.1.call-start
  50.5 31.3 %scatter_fusion.1 = f32[2,256,256]{2,1,0:T(8,128)S(1)} fusion(f32[2,256,256]{2,1,0:T(8,128)S(1)} %broadcast.145.clone.1, s32[512]{0:T(512)S(1)} %bitcast.126, f32[512]{0:T(512)S(1)} %bitcast.132), kind=kCustom, calls=%fused_computation.3 | custom fusion | flops 512 | bytes 12288 | tf_op jit(solution)/shard_map/scatter-add | solution.py:11
  81.8 0.6 iota_compare_fusion.1
  82.4 3.2 gather_fusion.1
  85.6 0.2 convolution_convert_fusion.4
  85.8 0.0 copy-start.1
  85.8 1.3 convolution_bitcast_fusion.2
  87.1 0.2 convolution_convert_fusion.6
  87.3 1.3 convolution_bitcast_fusion.3
  88.7 0.3 fusion.24
  89.0 0.4 multiply_reduce_fusion.3
  89.4 0.1 fusion.36
  89.6 0.2 broadcast_select_fusion
  89.8 0.3 convolution_convert_fusion.3
  90.1 1.0 convolution_convert_fusion.1
  91.1 34.1 %all-gather.8.cloned.1.call-done = f32[2048,512]{1,0:T(8,128)} async-done(((f32[256,512]{1,0:T(8,128)}), f32[2048,512]{1,0:T(8,128)}) %all-gather.8.cloned.1.call-update) | async-done | bytes 4194320 | tf_op jit(solution)/shard_map/all_gather | solution.py:65
  125.2 2.9 select_reduce_fusion
  128.1 0.3 fusion.21
  128.4 0.2 convolution_convert_fusion.2
  128.7 0.3 fusion.20
  129.0 0.2 convolution_convert_fusion
  129.2 0.3 convolution_bitcast_fusion
  129.6 0.3 convolution_bitcast_fusion.1
  130.0 2.4 pad_maximum_fusion
  132.4 5.5 %copy.25 = f32[4,512,512]{2,0,1:T(4,128)} copy(f32[4,512,512]{1,2,0:T(8,128)} %pad_maximum_fusion) | data formatting | bytes 8388608 | tf_op jit(solution)/shard_map/stack | solution.py:79
  137.8 6.2 %fusion.32 = f32[4,512,512]{2,0,1:T(4,128)S(1)} fusion(f32[4,512,512]{2,0,1:T(4,128)} %copy.25, s32[4]{0:T(128)S(1)} %bitcast.134), kind=kOutput, calls=%fused_computation.98 | convolution fusion | flops 50331664 | bytes 8388624 | tf_op jit(solution)/shard_map/sk,sde->kde/dot_general | solution.py:84
  144.0 3.2 copy.26
  147.3 0.0 reduce-scatter.2.cloned.1.call-update
  147.3 0.0 all-gather.10.cloned.1.call-start
  147.4 43.2 %reduce-scatter.2.cloned.1.call-done = f32[512,512]{1,0:T(8,128)} async-done(((f32[2048,512]{1,0:T(8,128)}), f32[512,512]{1,0:T(8,128)}) %reduce-scatter.2.cloned.1.call-update) | async-done | bytes 1048592 | tf_op jit(solution)/shard_map/reduce_scatter | solution.py:85
  190.5 0.0 all-gather.10.cloned.1.call-update
  190.6 21.1 %all-gather.1 = f32[8,1,256]{2,1,0:T(1,128)S(1)} all-gather(f32[1,1,256]{2,1,0:T(1,128)S(1)} %bitcast.135), channel_id=1, replica_groups=mesh['bucket'=8,'rel'=4] {'bucket'}, dimensions={0}, use_global_device_ids=true | all-gather | bytes 9216 | tf_op jit(solution)/shard_map/all_gather | solution.py:66
  211.7 0.1 fusion.26
  211.8 1.2 fusion.41
  213.0 1.3 multiply_reduce_fusion
  214.3 0.6 fusion.37
  214.9 0.3 fusion.25
  215.2 0.4 multiply_reduce_fusion.1
  215.6 0.6 fusion.38
  216.2 0.9 divide_subtract_fusion
  217.1 1.0 divide_subtract_fusion.1
  218.1 98.9 %all-gather.10.cloned.1.call-done = f32[4096,512]{1,0:T(8,128)} async-done(((f32[512,512]{1,0:T(8,128)}), f32[4096,512]{1,0:T(8,128)}) %all-gather.10.cloned.1.call-update) | async-done | bytes 8388624 | tf_op jit(solution)/shard_map/all_gather | solution.py:90
  317.1 5.5 %reduce_sum.69 = f32[512,512]{1,0:T(8,128)} reduce(f32[8,512,512]{2,1,0:T(8,128)} %bitcast.129, f32[]{:T(128)} %constant.15.clone.1), dimensions={0}, to_apply=%region_9.11 | reduce | flops 1835008 | bytes 9437188 | tf_op jit(solution)/shard_map/reduce_sum | solution.py:90
  (40 shorter events, 0.2 us)
Async XLA Ops:
  7.2 35.9 %copy-start.11 = (s32[1,1,4]{2,1,0:T(1,128)S(1)}, s32[1,1,4]{2,1,0:T(1,128)}, u32[]{:S(2)}) copy-start(s32[1,1,4]{2,1,0:T(1,128)} %param.18) | copy-start | bytes 52
  7.2 36.5 %all-gather.6.cloned.1.call-start = ((), (), s32[]{:S(2)}) async-start(), calls=%async_computation.1 | async-start | bytes 2621440 | tf_op jit(solution)/shard_map/all_gather | solution.py:109
  7.9 117.3 %all-gather.8.cloned.1.call-start = ((), (), s32[]{:S(2)}) async-start(), calls=%async_computation.2 | async-start | bytes 4718592 | tf_op jit(solution)/shard_map/all_gather | solution.py:65
  46.1 2.0 copy-start.17
  46.1 2.5 copy-start.6
  49.6 141.0 %reduce-scatter.2.cloned.1.call-start = ((), (), s32[]{:S(2)}) async-start(), calls=%async_computation.3 | async-start | bytes 5242880 | tf_op jit(solution)/shard_map/reduce_scatter | solution.py:85
  85.6 3.9 %copy-start.12 = (f32[256]{0:T(256)S(1)}, f32[256]{0:T(256)}, u32[]{:S(2)}) copy-start(f32[256]{0:T(256)} %param.14) | copy-start | bytes 3076
  85.6 3.9 %copy-start = (f32[256,512]{1,0:T(8,128)S(1)}, f32[256,512]{1,0:T(8,128)}, u32[]{:S(2)}) copy-start(f32[256,512]{1,0:T(8,128)} %param.13) | copy-start | bytes 1572868
  85.8 3.8 %copy-start.1 = (bf16[2,512,512]{2,1,0:T(8,128)(2,1)S(1)}, bf16[2,512,512]{2,1,0:T(8,128)(2,1)}, u32[]{:S(2)}) copy-start(bf16[2,512,512]{2,1,0:T(8,128)(2,1)} %gather_fusion.1) | copy-start | bytes 3145732
  85.8 3.8 %copy-start.16 = (pred[2]{0:T(512)(128)(4,1)S(1)}, pred[2]{0:T(512)(128)(4,1)}, u32[]{:S(2)}) copy-start(pred[2]{0:T(512)(128)(4,1)} %get-tuple-element.12) | copy-start | bytes 10
  88.7 36.5 %copy-start.14 = (pred[8]{0:T(512)(128)(4,1)S(1)}, pred[8]{0:T(512)(128)(4,1)}, u32[]{:S(2)}) copy-start(pred[8]{0:T(512)(128)(4,1)} %iota_compare_fusion.1) | copy-start | bytes 28
  89.6 35.6 %copy-start.4 = (bf16[256,512]{1,0:T(8,128)(2,1)}, bf16[256,512]{1,0:T(8,128)(2,1)S(1)}, u32[]{:S(2)}) copy-start(bf16[256,512]{1,0:T(8,128)(2,1)S(1)} %fusion.36) | copy-start | bytes 786436
  90.1 38.0 %copy-start.10 = (bf16[256,512]{1,0:T(8,128)(2,1)}, bf16[256,512]{1,0:T(8,128)(2,1)S(1)}, u32[]{:S(2)}) copy-start(bf16[256,512]{1,0:T(8,128)(2,1)S(1)} %convolution_convert_fusion.3) | copy-start | bytes 786436
  125.2 3.5 %copy-start.9 = (bf16[256,512]{1,0:T(8,128)(2,1)S(1)}, bf16[256,512]{1,0:T(8,128)(2,1)}, u32[]{:S(2)}) copy-start(bf16[256,512]{1,0:T(8,128)(2,1)} %convolution_convert_fusion.1) | copy-start | bytes 786436
  125.2 4.0 %copy-start.5 = (bf16[256,512]{1,0:T(8,128)(2,1)S(1)}, bf16[256,512]{1,0:T(8,128)(2,1)}, u32[]{:S(2)}) copy-start(bf16[256,512]{1,0:T(8,128)(2,1)} %copy-done.4) | copy-start | bytes 786436
  128.1 1.9 copy-start.2
  128.1 1.9 copy-start.3
  128.4 0.8 copy-start.7
  147.3 43.3 %copy-start.13 = (f32[256]{0:T(256)S(1)}, f32[256]{0:T(256)}, u32[]{:S(2)}) copy-start(f32[256]{0:T(256)} %get-tuple-element.11) | copy-start | bytes 3076
  147.3 64.4 %copy-start.15 = (pred[8]{0:T(512)(128)(4,1)S(1)}, pred[8]{0:T(512)(128)(4,1)}, u32[]{:S(2)}) copy-start(pred[8]{0:T(512)(128)(4,1)} %iota_compare_fusion.1) | copy-start | bytes 28
  147.3 64.5 %copy-start.8 = (bf16[256,256]{1,0:T(8,128)(2,1)S(1)}, bf16[256,256]{1,0:T(8,128)(2,1)}, u32[]{:S(2)}) copy-start(bf16[256,256]{1,0:T(8,128)(2,1)} %copy-done.7) | copy-start | bytes 393220
  147.3 169.8 %all-gather.10.cloned.1.call-start = ((), (), s32[]{:S(2)}) async-start(), calls=%async_computation.4 | async-start | bytes 9437184 | tf_op jit(solution)/shard_map/all_gather | solution.py:90
Sparse Core Ops, SparseCore 0:
  9.5 25.2 all-gather.5
  49.7 75.4 all-gather.7
  147.4 43.0 reduce-scatter.1
  192.5 124.4 all-gather.9
